TPU v7x, 256 devices: a whole 4x4x8 slice. The times are simulated.
256 devices in a mesh: dp: 32 (over z, x), mp: 8 (over y, core).
Axes of the slice: x: 4, y: 4, z: 8, core: 2. Of those that a mesh axis runs over, the one named last changes fastest.
Arguments:
- token_ids: int32 [2048, 7], replicated, may hold values from 0 to 65535
- lengths: int32 [2048], replicated, may hold values from 1 to 7, as said below
- pack_dest: int32 [2048], replicated, may hold values from 0 to 31, as said below
- ref_hidden: bfloat16 [2048, 7, 4096], P('dp', None, 'mp'), may hold values from -45 to 45
- reward_hidden: bfloat16 [2048, 7, 4096], P('dp', None, 'mp'), may hold values from -140 to 140
- head_weight: bfloat16 [4096, 65536], P('mp', 'dp'), may hold values from -0.25 to 0.25
- norm_gain: float32 [4096], P('mp'), may hold values from 0.1 to 1.9
- score_weight: float32 [4096], P('mp'), may hold values from -0.09375 to 0.09375
- value_weight: float32 [4096], P('mp'), may hold values from -0.09375 to 0.09375
- old_logprob: float32 [8192], P('dp'), may hold values from -14 to -1
Outputs:
- ref_logprob: float32 [8192], P('dp')
- advantage: float32 [8192], P('dp')
Inputs may be any that keep to these rules, and one draw needn't show every extreme that they name: `pack_dest`: request i belongs to request shard i // 64. Each request shard sends exactly 2 of its requests to every packed shard. A packed shard lists its requests by request shard, then by request index, and packs their tokens in that order from slot 0. In that order the requests of a packed shard form pairs whose lengths sum to 8, so every packed shard holds exactly 256 tokens; every packed shard has a request of length 1 and one of length 7.
All inputs are finite; a program needn't handle non-finite values.
Results may differ from a plain program's by a relative error of at most 0.0003.
Values may be sent and summed in bfloat16 or wider, within the bound.
No kernel may reach another device: no remote copies, remote signals or barrier semaphores. Data moves between devices by JAX's collectives and lax.ppermute only.
A program may use at most 192 MiB of HBM per device.

v0:
```python
import jax
import jax.numpy as jnp
from jax import lax
from jax.sharding import PartitionSpec as P

kl_coef = 0.1
discount = 0.99
gae_mix = 0.95
norm_eps = 1e-05


def pair_rank(dest):
    count = dest.shape[-1]
    idx = jnp.arange(count, dtype=jnp.int32)
    same = dest[..., None, :] == dest[..., :, None]
    earlier = idx[None, :] < idx[:, None]
    return jnp.sum(jnp.logical_and(same, earlier).astype(jnp.int32), axis=-1)


def body(
    token_ids,
    lengths,
    pack_dest,
    ref_hidden,
    reward_hidden,
    head_weight,
    norm_gain,
    score_weight,
    value_weight,
    old_logprob,
):
    shards = lax.axis_size("dp")
    ways = lax.axis_size("mp")
    me = lax.axis_index("dp")
    part = lax.axis_index("mp")
    req_dev, max_len, width_dev = ref_hidden.shape
    pair_len = max_len + 1
    slot_dev = shards * pair_len
    sub_len = slot_dev // ways
    blocks = sub_len // pair_len
    width_full = width_dev * ways
    steps = jnp.arange(max_len, dtype=jnp.int32)
    dest = lax.dynamic_slice_in_dim(pack_dest, me * req_dev, req_dev)
    size = lax.dynamic_slice_in_dim(lengths, me * req_dev, req_dev)
    rank = pair_rank(dest)
    row = dest[:, None] * pair_len + steps[None, :] + rank[:, None] * (pair_len - size[:, None])
    row = jnp.where(steps[None, :] < size[:, None], row, -1).reshape(-1)
    onehot = (row[None, :] == jnp.arange(slot_dev, dtype=jnp.int32)[:, None]).astype(jnp.bfloat16)
    ref_send = jnp.dot(
        onehot, ref_hidden.reshape(req_dev * max_len, width_dev), preferred_element_type=jnp.float32
    ).astype(jnp.bfloat16)
    reward_send = jnp.dot(
        onehot,
        reward_hidden.reshape(req_dev * max_len, width_dev),
        preferred_element_type=jnp.float32,
    ).astype(jnp.bfloat16)
    send = jnp.concatenate([ref_send, reward_send], axis=1).reshape(shards, pair_len, 2 * width_dev)
    got = lax.all_to_all(send, "dp", 0, 0, tiled=True).reshape(slot_dev, 2 * width_dev)
    ref_packed = got[:, :width_dev]
    reward_packed = got[:, width_dev:]
    own_rows = lax.all_to_all(
        ref_packed.reshape(ways, sub_len, width_dev), "mp", 0, 2, tiled=True
    ).reshape(sub_len, width_full)
    block_rows = lax.all_gather(own_rows, "dp", axis=0, tiled=True)
    weight = lax.all_gather(head_weight, "mp", axis=0, tiled=True)
    first_src = part * blocks
    dest4 = lax.dynamic_slice_in_dim(pack_dest, first_src * req_dev, blocks * req_dev).reshape(
        blocks, req_dev
    )
    size4 = lax.dynamic_slice_in_dim(lengths, first_src * req_dev, blocks * req_dev).reshape(
        blocks, req_dev
    )
    tok4 = lax.dynamic_slice_in_dim(token_ids, first_src * req_dev, blocks * req_dev, axis=0)
    rank4 = pair_rank(dest4)
    key = (
        dest4[:, :, None] * sub_len
        + jnp.arange(blocks, dtype=jnp.int32)[:, None, None] * pair_len
        + steps[None, None, :]
        + rank4[:, :, None] * (pair_len - size4[:, :, None])
    )
    key = jnp.where(steps[None, None, :] < size4[:, :, None], key, -1).reshape(-1)
    hits = key[None, :] == jnp.arange(shards * sub_len, dtype=jnp.int32)[:, None]
    targets = jnp.sum(jnp.where(hits, tok4.reshape(-1)[None, :], 0), axis=1)
    logits = jnp.dot(block_rows, weight, preferred_element_type=jnp.float32)
    vocab_dev = head_weight.shape[1]
    row_max = jnp.max(logits, axis=1)
    exp_total = jnp.sum(jnp.exp(logits - row_max[:, None]), axis=1)
    column = jnp.arange(vocab_dev, dtype=jnp.int32)[None, :] + me * vocab_dev
    target_logit = jnp.sum(jnp.where(column == targets[:, None], logits, 0.0), axis=1)
    stats = jnp.stack([row_max, exp_total, target_logit]).reshape(3, shards, sub_len)
    stats = lax.all_to_all(stats, "dp", 1, 1, tiled=True)
    joint_max = jnp.max(stats[0], axis=0)
    joint_total = jnp.sum(stats[1] * jnp.exp(stats[0] - joint_max[None, :]), axis=0)
    joint_target = jnp.sum(stats[2], axis=0)
    block_logprob = joint_target - joint_max - jnp.log(joint_total)
    ref_logprob = lax.all_gather(block_logprob, "mp", axis=0, tiled=True)
    hidden_f = reward_packed.astype(jnp.float32)
    sums = jnp.stack(
        [
            jnp.sum(hidden_f * hidden_f, axis=1),
            jnp.sum(hidden_f * (norm_gain * score_weight), axis=1),
            jnp.sum(hidden_f * (norm_gain * value_weight), axis=1),
        ]
    )
    squares, score_dot, value_dot = lax.psum(sums, "mp")
    inv_rms = lax.rsqrt(squares / width_full + norm_eps)
    score = score_dot * inv_rms
    value_est = value_dot * inv_rms
    mine = (pack_dest.reshape(shards, req_dev) == me).astype(jnp.int32)
    is_first = jnp.logical_and(mine == 1, jnp.cumsum(mine, axis=1) == 1)
    first_len = jnp.sum(jnp.where(is_first, lengths.reshape(shards, req_dev), 0), axis=1)
    place = jnp.arange(pair_len, dtype=jnp.int32)[None, :]
    is_last = jnp.logical_or(place == first_len[:, None] - 1, place == pair_len - 1)
    is_last_flat = is_last.reshape(-1)
    reward = -kl_coef * (old_logprob - ref_logprob) + jnp.where(is_last_flat, score, 0.0)
    next_value = jnp.concatenate([value_est[1:], jnp.zeros((1,), jnp.float32)])
    not_last = 1.0 - is_last_flat.astype(jnp.float32)
    td_error = (reward + discount * next_value * not_last - value_est).reshape(shards, pair_len)
    decay = discount * gae_mix
    carry = td_error[:, pair_len - 1]
    columns = [carry]
    for step in range(pair_len - 2, -1, -1):
        carry = td_error[:, step] + decay * jnp.where(is_last[:, step], 0.0, carry)
        columns.append(carry)
    advantage = jnp.stack(columns[::-1], axis=1).reshape(-1)
    return (ref_logprob, advantage)


def solution(mesh):
    return jax.shard_map(
        body,
        mesh=mesh,
        in_specs=(
            P(),
            P(),
            P(),
            P("dp", None, "mp"),
            P("dp", None, "mp"),
            P("mp", "dp"),
            P("mp"),
            P("mp"),
            P("mp"),
            P("dp"),
        ),
        out_specs=(P("dp"), P("dp")),
        check_vma=False,
    )
```

profile of v0, /device:TPU:1, one launch (start us, length us, event | category | flops | bytes accessed | tf_op | source)
XLA Modules:
  0.0 304.3 jit_solution(12371459190618607233)
XLA Ops:
  7.3 0.8 broadcast_multiply_fusion
  8.1 0.2 convert_reduce_fusion.1
  8.2 0.8 subtract_multiply_fusion.1
  9.1 0.1 select_n.99
  9.3 1.3 copy.33
  10.5 0.2 reshape.220
  10.7 1.3 copy.34
  12.0 0.2 reshape.221
  12.2 0.3 convolution_convert_fusion.1
  12.5 0.3 convolution_convert_fusion
  12.9 27.9 %all_to_all.25 = bf16[32,8,1024]{2,1,0:T(8,128)(2,1)S(1)} all-to-all(bf16[32,8,1024]{2,1,0:T(8,128)(2,1)S(1)} %maximum_bitcast_fusion), channel_id=1, replica_groups=mesh['dp'=32,'mp'=8] {'dp'}, dimensions={0} | all-to-all | bytes 1048576 | tf_op jit(solution)/shard_map/all_to_all | solution.py:58
  40.8 13.2 %all_to_all.26 = bf16[8,32,512]{2,1,0:T(8,128)(2,1)S(1)} all-to-all(bf16[8,32,512]{2,1,0:T(8,128)(2,1)S(1)} %bitcast.31), channel_id=1, replica_groups=mesh['dp'=32,'mp'=8] {'mp'}, dimensions={0} | all-to-all | bytes 524288 | tf_op jit(solution)/shard_map/all_to_all | solution.py:61
  54.0 0.7 copy.39
  54.8 0.7 all-gather.5.cloned.1.call-update
  56.0 0.2 reduce_window_sum.11
  56.7 0.2 broadcast_in_dim.45
  56.9 0.2 convert_reduce_fusion
  57.2 0.2 add_select_fusion
  57.4 0.2 select_n.102
  57.6 0.6 dynamic-slice
  58.9 0.8 select_reduce_fusion.1
  59.7 0.2 fusion
  59.9 86.8 %all-gather.3.cloned.1.call-done = bf16[1024,4096]{1,0:T(8,128)(2,1)} async-done(((bf16[32,4096]{1,0:T(8,128)(2,1)}), bf16[1024,4096]{1,0:T(8,128)(2,1)}) %all-gather.3.cloned.1.call-update) | async-done | bytes 8388624 | tf_op jit(solution)/shard_map/all_gather | solution.py:64
  146.7 87.6 %all-gather.5.cloned.1.call-done = bf16[4096,2048]{1,0:T(8,128)(2,1)} async-done(((bf16[512,2048]{1,0:T(8,128)(2,1)}), bf16[4096,2048]{1,0:T(8,128)(2,1)}) %all-gather.5.cloned.1.call-update) | async-done | bytes 16777232 | tf_op jit(solution)/shard_map/all_gather | solution.py:65
  234.3 24.2 %fusion.12 = (f32[1024]{0:T(1024)S(1)}, f32[1024,2048]{1,0:T(8,128)}) fusion(bf16[1024,4096]{1,0:T(8,128)(2,1)} %all-gather.3.cloned.1.call-done, bf16[4096,2048]{1,0:T(8,128)(2,1)} %all-gather.5.cloned.1.call-done), kind=kOutput, calls=%fused_computation.58 | convolution fusion | flops 17181966336 | bytes 33558528 | tf_op jit(solution)/shard_map/dot_general | solution.py:84
  258.6 4.7 %exponential_reduce_fusion = (f32[1024]{0:T(1024)S(1)}, f32[1024]{0:T(1024)S(1)}) fusion(f32[1024,2048]{1,0:T(8,128)} %get-tuple-element.29, f32[1024]{0:T(1024)S(1)} %get-tuple-element.28, s32[1024]{0:T(1024)S(1)} %select_reduce_fusion.1, s32[2048]{0:T(1024)S(1)} %iota_add_fusion), kind=kLoop, calls=%fused_computation.1 | loop fusion | flops 10483712 | bytes 8413184 | tf_op jit(solution)/shard_map/reduce_sum | solution.py:87
  263.4 0.7 pad_maximum_fusion
  264.1 9.5 %all-to-all-start.2 = ((f32[3,32,32]{2,0,1:T(4,128)}), f32[3,32,32]{2,0,1:T(4,128)S(1)}, u32[]{:S(2)}, u32[]{:S(2)}) async-start(f32[3,32,32]{2,0,1:T(4,128)} %pad_maximum_fusion), calls=%async_computation.2 | async-start | bytes 131072 | tf_op jit(solution)/shard_map/all_to_all | solution.py:91
  273.6 8.9 %all-to-all-done.2 = f32[3,32,32]{2,0,1:T(4,128)S(1)} async-done(((f32[3,32,32]{2,0,1:T(4,128)}), f32[3,32,32]{2,0,1:T(4,128)S(1)}, u32[]{:S(2)}, u32[]{:S(2)}) %all-to-all-start.2) | async-done | bytes 12320 | tf_op jit(solution)/shard_map/all_to_all | solution.py:91
  282.7 13.6 %all-reduce.1 = (f32[256]{0:T(256)S(1)}, f32[3,256]{1,0:T(4,128)S(1)}) all-reduce(f32[256]{0:T(256)S(1)} %subtract_dynamic-update-slice_fusion, f32[3,256]{1,0:T(4,128)S(1)} %pad_maximum_fusion.1), channel_id=1, replica_groups=mesh['dp'=32,'mp'=8] {'mp'}, use_global_device_ids=true, to_apply=%add | all-reduce | flops 1024 | bytes 8192
  296.6 0.1 slice_add_fusion.6
  296.8 0.7 reshape.228
  (57 shorter events, 2.1 us)
Async XLA Ops:
  7.2 49.3 %copy-start = (s32[2048,7]{0,1:T(8,128)S(1)}, s32[2048,7]{0,1:T(8,128)}, u32[]{:S(2)}) copy-start(s32[2048,7]{0,1:T(8,128)} %param.10) | copy-start | bytes 172036
  7.2 50.4 %copy-start.8 = (u32[256]{0:T(256)S(1)}, u32[256]{0:T(256)}, u32[]{:S(2)}) copy-start(u32[256]{0:T(256)} %constant.56) | copy-start | bytes 3076
  7.2 48.4 %copy-start.2 = (s32[2048]{0:T(1024)S(1)}, s32[2048]{0:T(1024)}, u32[]{:S(2)}) copy-start(s32[2048]{0:T(1024)} %param.12) | copy-start | bytes 24580
  7.2 48.3 %copy-start.1 = (s32[2048]{0:T(1024)S(1)}, s32[2048]{0:T(1024)}, u32[]{:S(2)}) copy-start(s32[2048]{0:T(1024)} %param.11) | copy-start | bytes 24580
  7.2 51.6 %copy-start.5 = (f32[512]{0:T(512)S(1)}, f32[512]{0:T(512)}, u32[]{:S(2)}) copy-start(f32[512]{0:T(512)} %param.18) | copy-start | bytes 6148
  7.2 51.6 %copy-start.4 = (f32[512]{0:T(512)S(1)}, f32[512]{0:T(512)}, u32[]{:S(2)}) copy-start(f32[512]{0:T(512)} %param.17) | copy-start | bytes 6148
  7.2 51.6 %copy-start.3 = (f32[512]{0:T(512)S(1)}, f32[512]{0:T(512)}, u32[]{:S(2)}) copy-start(f32[512]{0:T(512)} %param.16) | copy-start | bytes 6148
  7.2 139.5 %all-gather.3.cloned.1.call-start = ((), (), s32[]{:S(2)}) async-start(), calls=%async_computation.3 | async-start | bytes 8650752 | tf_op jit(solution)/shard_map/all_gather | solution.py:64
  54.7 179.6 %all-gather.5.cloned.1.call-start = ((), (), s32[]{:S(2)}) async-start(), calls=%async_computation.4 | async-start | bytes 18874368 | tf_op jit(solution)/shard_map/all_gather | solution.py:65
  258.5 37.9 %copy-start.6 = (f32[256]{0:T(256)S(1)}, f32[256]{0:T(256)}, u32[]{:S(2)}) copy-start(f32[256]{0:T(256)} %param.19) | copy-start | bytes 3076
  264.1 18.4 %all-to-all-start.2 = ((f32[3,32,32]{2,0,1:T(4,128)}), f32[3,32,32]{2,0,1:T(4,128)S(1)}, u32[]{:S(2)}, u32[]{:S(2)}) async-start(f32[3,32,32]{2,0,1:T(4,128)} %pad_maximum_fusion), calls=%async_computation.2 | async-start | bytes 131072 | tf_op jit(solution)/shard_map/all_to_all | solution.py:91
  296.3 1.2 copy-start.7
Sparse Core Ops, SparseCore 0:
  54.8 91.8 all-gather.2
  148.6 85.6 all-gather.4
where the time goes:
time: 305 us; the launch traced here: 304 us
  waiting for transfers between devices  184 us (60%)
  blocking collectives  54.7 us (18%)
  matrix products  24.8 us (8%)
  between operations  15 us (5%)
  starting transfers between devices  9.61 us (3%)
  other arithmetic  9.59 us (3%)
  local copies, waits for them, and re-layouts  6.68 us (2%)
    all_gather x1, waiting for transfers between devices, body(): weight = lax.all_gather(head_weight, 'mp', axis=0, tiled=True)  87.6 us
    all_gather x1, waiting for transfers between devices, body(): block_rows = lax.all_gather(own_rows, 'dp', axis=0, tiled=True)  86.8 us
    all_to_all x1, blocking collectives, body(): lax.all_to_all(send, 'dp', 0, 0, tiled=True)  27.9 us
    dot_general x1, matrix products, body(): logits = jnp.dot(block_rows, weight, preferred_element_type=jnp.float32)  24.2 us
    unnamed x1, blocking collectives  13.6 us
    all_to_all x1, blocking collectives, body(): lax.all_to_all(ref_packed.reshape(ways, sub_len, width_dev), 'mp', 0, 2,...  13.2 us
    all_to_all x1, starting transfers between devices, body(): stats = lax.all_to_all(stats, 'dp', 1, 1, tiled=True)  9.53 us
    all_to_all x1, waiting for transfers between devices, body(): stats = lax.all_to_all(stats, 'dp', 1, 1, tiled=True)  8.86 us
  transfers between devices with their start and end apart: 3, of which 3 were waited for; matrix products, arithmetic and copies ran while one was open for 1% of the time, Pallas kernels for 0%

commit v1 on v0

--- a/solution.py
+++ b/solution.py
@@ -7,6 +7,22 @@
 discount = 0.99
 gae_mix = 0.95
 norm_eps = 1e-05
+
+
+def ring_gather(x, axis, dim):
+    ways, here, hop = (lax.axis_size(axis), lax.axis_index(axis), x.shape[dim])
+    shape = [n * ways if d == dim else n for d, n in enumerate(x.shape)]
+    full = lax.dynamic_update_slice_in_dim(jnp.zeros(shape, x.dtype), x, here * hop, axis=dim)
+    going_up = going_down = x
+    for far in range(1, ways // 2 + 1):
+        going_up = lax.ppermute(going_up, axis, [(d, (d + 1) % ways) for d in range(ways)])
+        full = lax.dynamic_update_slice_in_dim(full, going_up, (here - far) % ways * hop, axis=dim)
+        if 2 * far < ways:
+            going_down = lax.ppermute(going_down, axis, [(d, (d - 1) % ways) for d in range(ways)])
+            full = lax.dynamic_update_slice_in_dim(
+                full, going_down, (here + far) % ways * hop, axis=dim
+            )
+    return full
 
 
 def pair_rank(dest):
@@ -62,7 +78,7 @@
         ref_packed.reshape(ways, sub_len, width_dev), "mp", 0, 2, tiled=True
     ).reshape(sub_len, width_full)
     block_rows = lax.all_gather(own_rows, "dp", axis=0, tiled=True)
-    weight = lax.all_gather(head_weight, "mp", axis=0, tiled=True)
+    weight = ring_gather(head_weight, "mp", 0)
     first_src = part * blocks
     dest4 = lax.dynamic_slice_in_dim(pack_dest, first_src * req_dev, blocks * req_dev).reshape(
         blocks, req_dev

time: 305 us -> 232 us (0.76)
  waiting for transfers between devices: 184 us -> 65.8 us
  local copies, waits for them, and re-layouts: 6.68 us -> 35.7 us
  starting transfers between devices: 9.61 us -> 17.6 us
  blocking collectives: 54.7 us -> 61.6 us
    all_gather x1 -> x0, waiting for transfers between devices: 87.6 us -> none  [body(): weight = lax.all_gather(head_weight, 'mp', axis=0, tiled=True)]
    all_gather x1, waiting for transfers between devices: 86.8 us -> 0.01 us  [body(): block_rows = lax.all_gather(own_rows, 'dp', axis=0, tiled=True)]
    ppermute x0 -> x7, waiting for transfers between devices: none -> 57 us  [the longest x4 56.7 us: ring_gather(): lax.ppermute(going_up, axis, [(d, (d + 1) % ways) for d in range(ways)])]
    dynamic_update_slice x0 -> x8, local copies, waits for them, and re-layouts: none -> 22.3 us  [the longest x4 11.1 us: ring_gather(): lax.dynamic_update_slice_in_dim(full, going_up, (here - far) % ways * hop...]
    ppermute x0 -> x7, starting transfers between devices: none -> 13.1 us  [the longest x4 8.77 us: ring_gather(): lax.ppermute(going_up, axis, [(d, (d + 1) % ways) for d in range(ways)])]
    unnamed x1, blocking collectives: 13.6 us -> 20.5 us
    broadcast_in_dim x0 -> x1, local copies, waits for them, and re-layouts: none -> 6.02 us  [ring_gather(): jnp.zeros(shape, x.dtype)]
    all_to_all x1, starting transfers between devices: 9.53 us -> 4.38 us  [body(): stats = lax.all_to_all(stats, 'dp', 1, 1, tiled=True)]
  transfers between devices with their start and end apart: 3 -> 9, of which waited for: 3 -> 6; matrix products, arithmetic and copies ran while one was open for 1% -> 14% of each run, Pallas kernels for 0% -> 0%
where the time goes in v1:
time: 232 us; the launch traced here: 231 us
  waiting for transfers between devices  65.8 us (28%)
  blocking collectives  61.6 us (27%)
  local copies, waits for them, and re-layouts  35.7 us (15%)
  matrix products  25.8 us (11%)
  starting transfers between devices  17.6 us (8%)
  between operations  15.1 us (7%)
  other arithmetic  9.71 us (4%)
    ppermute x4, waiting for transfers between devices, ring_gather(): lax.ppermute(going_up, axis, [(d, (d + 1) % ways) for d in range(ways)])  56.7 us
    all_to_all x1, blocking collectives, body(): lax.all_to_all(send, 'dp', 0, 0, tiled=True)  27.9 us
    dot_general x1, matrix products, body(): logits = jnp.dot(block_rows, weight, preferred_element_type=jnp.float32)  24.2 us
    unnamed x1, blocking collectives  20.5 us
    all_to_all x1, blocking collectives, body(): lax.all_to_all(ref_packed.reshape(ways, sub_len, width_dev), 'mp', 0, 2,...  13.2 us
    dynamic_update_slice x4, local copies, waits for them, and re-layouts, ring_gather(): lax.dynamic_update_slice_in_dim(full, going_up, (here - far) % ways * hop...  11.1 us
    dynamic_update_slice x3, local copies, waits for them, and re-layouts, ring_gather(): lax.dynamic_update_slice_in_dim(full, going_down, (here + far) % ways * h...  9.62 us
    all_to_all x1, waiting for transfers between devices, body(): stats = lax.all_to_all(stats, 'dp', 1, 1, tiled=True)  8.8 us
  transfers between devices with their start and end apart: 9, of which 6 were waited for; matrix products, arithmetic and copies ran while one was open for 14% of the time, Pallas kernels for 0%

profile of v1, /device:TPU:1, one launch (start us, length us, event | category | flops | bytes accessed | tf_op | source)
XLA Modules:
  0.0 231.3 jit_solution(8120368279451345760)
XLA Ops:
  7.3 0.9 broadcast_multiply_fusion
  9.4 1.3 copy.33
  10.8 1.3 copy.34
  12.1 0.9 reshape.221
  13.4 1.3 convolution_convert_fusion
  14.8 27.9 %all_to_all.25 = bf16[32,8,1024]{2,1,0:T(8,128)(2,1)S(1)} all-to-all(bf16[32,8,1024]{2,1,0:T(8,128)(2,1)S(1)} %maximum_bitcast_fusion), channel_id=1, replica_groups=mesh['dp'=32,'mp'=8] {'dp'}, dimensions={0} | all-to-all | bytes 1048576 | tf_op jit(solution)/shard_map/all_to_all | solution.py:74
  42.7 13.2 %all_to_all.26 = bf16[8,32,512]{2,1,0:T(8,128)(2,1)S(1)} all-to-all(bf16[8,32,512]{2,1,0:T(8,128)(2,1)S(1)} %bitcast.31), channel_id=1, replica_groups=mesh['dp'=32,'mp'=8] {'mp'}, dimensions={0} | all-to-all | bytes 524288 | tf_op jit(solution)/shard_map/all_to_all | solution.py:77
  56.6 1.2 collective-permute-start
  57.9 23.0 %collective-permute-done = bf16[512,2048]{1,0:T(8,128)(2,1)S(1)} collective-permute-done((bf16[512,2048]{1,0:T(8,128)(2,1)S(1)}, bf16[512,2048]{1,0:T(8,128)(2,1)S(1)}, u32[]{:S(2)}, u32[]{:S(2)}) %collective-permute-start) | collective-permute-done | bytes 2097184 | tf_op jit(solution)/shard_map/ppermute | solution.py:18
  80.8 2.5 %collective-permute-start.2 = (bf16[512,2048]{1,0:T(8,128)(2,1)S(1)}, bf16[512,2048]{1,0:T(8,128)(2,1)}, u32[]{:S(2)}, u32[]{:S(2)}) collective-permute-start(bf16[512,2048]{1,0:T(8,128)(2,1)S(1)} %collective-permute-done), channel_id=1, source_target_pairs={{0,1},{1,2},{2,3},{3,4},{4,5},{5,6},{6,7},{7,0},{8,9},{9,10},{10,1... | collective-permute-start | bytes 6291464 | tf_op jit(solution)/shard_map/ppermute | solution.py:18
  83.6 2.1 collective-permute-start.3
  85.7 20.6 %collective-permute-done.2 = bf16[512,2048]{1,0:T(8,128)(2,1)} collective-permute-done((bf16[512,2048]{1,0:T(8,128)(2,1)S(1)}, bf16[512,2048]{1,0:T(8,128)(2,1)}, u32[]{:S(2)}, u32[]{:S(2)}) %collective-permute-start.2) | collective-permute-done | bytes 2097184 | tf_op jit(solution)/shard_map/ppermute | solution.py:18
  106.3 2.6 %collective-permute-start.4 = (bf16[512,2048]{1,0:T(8,128)(2,1)}, bf16[512,2048]{1,0:T(8,128)(2,1)}, u32[]{:S(2)}, u32[]{:S(2)}) collective-permute-start(bf16[512,2048]{1,0:T(8,128)(2,1)} %collective-permute-done.2), channel_id=1, source_target_pairs={{0,1},{1,2},{2,3},{3,4},{4,5},{5,6},{6,7},{7,0},{8,9},{9,10},{10,1... | collective-permute-start | bytes 6291464 | tf_op jit(solution)/shard_map/ppermute | solution.py:18
  110.4 2.3 collective-permute-start.5
  112.6 6.0 %broadcast_in_dim.46 = bf16[4096,2048]{1,0:T(8,128)(2,1)} broadcast(bf16[]{:T(256)} %constant.84.clone.1), dimensions={} | broadcast | bytes 16777218 | tf_op jit(solution)/shard_map/broadcast_in_dim | solution.py:15
  118.7 1.5 constant_dynamic-update-slice_fusion.7
  120.2 12.0 %collective-permute-done.4 = bf16[512,2048]{1,0:T(8,128)(2,1)} collective-permute-done((bf16[512,2048]{1,0:T(8,128)(2,1)}, bf16[512,2048]{1,0:T(8,128)(2,1)}, u32[]{:S(2)}, u32[]{:S(2)}) %collective-permute-start.4) | collective-permute-done | bytes 2097184 | tf_op jit(solution)/shard_map/ppermute | solution.py:18
  132.2 2.5 %collective-permute-start.6 = (bf16[512,2048]{1,0:T(8,128)(2,1)}, bf16[512,2048]{1,0:T(8,128)(2,1)S(1)}, u32[]{:S(2)}, u32[]{:S(2)}) collective-permute-start(bf16[512,2048]{1,0:T(8,128)(2,1)} %collective-permute-done.4), channel_id=1, source_target_pairs={{0,1},{1,2},{2,3},{3,4},{4,5},{5,6},{6,7},{7,0},{8,9},{9,10},{10,1... | collective-permute-start | bytes 6291464 | tf_op jit(solution)/shard_map/ppermute | solution.py:18
  136.6 0.8 select_reduce_fusion.1
  137.6 3.2 %constant_dynamic-update-slice_fusion.6 = bf16[4096,2048]{1,0:T(8,128)(2,1)} fusion(bf16[4096,2048]{1,0:T(8,128)(2,1)} %constant_dynamic-update-slice_fusion.7, bf16[512,2048]{1,0:T(8,128)(2,1)} %copy-done.2, s32[]{:T(128)S(6)} %select_n.157), kind=kLoop, calls=%fused_computation.46 | loop fusion | bytes 4194308 | tf_op jit(solution)/shard_map/dynamic_update_slice | solution.py:19
  140.8 3.2 %constant_dynamic-update-slice_fusion.5 = bf16[4096,2048]{1,0:T(8,128)(2,1)} fusion(bf16[4096,2048]{1,0:T(8,128)(2,1)} %constant_dynamic-update-slice_fusion.6, bf16[512,2048]{1,0:T(8,128)(2,1)} %collective-permute-done.1, s32[]{:T(128)S(6)} %select_n.159), kind=kLoop, calls=%fused_computation.45 | loop fusion | bytes 4194308 | tf_op jit(solution)/shard_map/dynamic_update_slice | solution.py:22
  144.0 3.2 %constant_dynamic-update-slice_fusion.4 = bf16[4096,2048]{1,0:T(8,128)(2,1)} fusion(bf16[4096,2048]{1,0:T(8,128)(2,1)} %constant_dynamic-update-slice_fusion.5, bf16[512,2048]{1,0:T(8,128)(2,1)} %collective-permute-done.2, s32[]{:T(128)S(6)} %select_n.161), kind=kLoop, calls=%fused_computation.44 | loop fusion | bytes 4194308 | tf_op jit(solution)/shard_map/dynamic_update_slice | solution.py:19
  147.2 3.2 %constant_dynamic-update-slice_fusion.3 = bf16[4096,2048]{1,0:T(8,128)(2,1)} fusion(bf16[4096,2048]{1,0:T(8,128)(2,1)} %constant_dynamic-update-slice_fusion.4, bf16[512,2048]{1,0:T(8,128)(2,1)} %collective-permute-done.3, s32[]{:T(128)S(6)} %select_n.163), kind=kLoop, calls=%fused_computation.43 | loop fusion | bytes 4194308 | tf_op jit(solution)/shard_map/dynamic_update_slice | solution.py:22
  150.4 3.2 %constant_dynamic-update-slice_fusion.2 = bf16[4096,2048]{1,0:T(8,128)(2,1)} fusion(bf16[4096,2048]{1,0:T(8,128)(2,1)} %constant_dynamic-update-slice_fusion.3, bf16[512,2048]{1,0:T(8,128)(2,1)} %collective-permute-done.4, s32[]{:T(128)S(6)} %select_n.165), kind=kLoop, calls=%fused_computation.42 | loop fusion | bytes 4194308 | tf_op jit(solution)/shard_map/dynamic_update_slice | solution.py:19
  153.6 3.2 %constant_dynamic-update-slice_fusion.1 = bf16[4096,2048]{1,0:T(8,128)(2,1)} fusion(bf16[4096,2048]{1,0:T(8,128)(2,1)} %constant_dynamic-update-slice_fusion.2, bf16[512,2048]{1,0:T(8,128)(2,1)} %collective-permute-done.5, s32[]{:T(128)S(6)} %select_n.167), kind=kLoop, calls=%fused_computation.41 | loop fusion | bytes 4194308 | tf_op jit(solution)/shard_map/dynamic_update_slice | solution.py:22
  156.8 1.1 collective-permute-done.6
  158.0 1.5 constant_dynamic-update-slice_fusion
  159.5 24.2 %fusion.12 = (f32[1024]{0:T(1024)S(1)}, f32[1024,2048]{1,0:T(8,128)}) fusion(bf16[1024,4096]{1,0:T(8,128)(2,1)} %all-gather.2.cloned.1.call-done, bf16[4096,2048]{1,0:T(8,128)(2,1)} %constant_dynamic-update-slice_fusion), kind=kOutput, calls=%fused_computation.66 | convolution fusion | flops 17181966336 | bytes 33558528 | tf_op jit(solution)/shard_map/dot_general | solution.py:100
  183.8 4.6 %exponential_reduce_fusion = (f32[1024]{0:T(1024)S(1)}, f32[1024]{0:T(1024)S(1)}) fusion(f32[1024,2048]{1,0:T(8,128)} %get-tuple-element.29, f32[1024]{0:T(1024)S(1)} %get-tuple-element.28, s32[1024]{0:T(1024)S(1)} %select_reduce_fusion.1, s32[2048]{0:T(1024)S(1)} %iota_add_fusion), kind=kLoop, calls=%fused_computation.1 | loop fusion | flops 10483712 | bytes 8413184 | tf_op jit(solution)/shard_map/reduce_sum | solution.py:103
  189.3 4.4 %all-to-all-start.2 = ((f32[3,32,32]{2,0,1:T(4,128)}), f32[3,32,32]{2,0,1:T(4,128)S(1)}, u32[]{:S(2)}, u32[]{:S(2)}) async-start(f32[3,32,32]{2,0,1:T(4,128)} %pad_maximum_fusion), calls=%async_computation.2 | async-start | bytes 131072 | tf_op jit(solution)/shard_map/all_to_all | solution.py:107
  193.7 8.8 %all-to-all-done.2 = f32[3,32,32]{2,0,1:T(4,128)S(1)} async-done(((f32[3,32,32]{2,0,1:T(4,128)}), f32[3,32,32]{2,0,1:T(4,128)S(1)}, u32[]{:S(2)}, u32[]{:S(2)}) %all-to-all-start.2) | async-done | bytes 12320 | tf_op jit(solution)/shard_map/all_to_all | solution.py:107
  202.7 20.5 %all-reduce.1 = (f32[256]{0:T(256)S(1)}, f32[3,256]{1,0:T(4,128)S(1)}) all-reduce(f32[256]{0:T(256)S(1)} %subtract_dynamic-update-slice_fusion, f32[3,256]{1,0:T(4,128)S(1)} %pad_maximum_fusion.1), channel_id=1, replica_groups=mesh['dp'=32,'mp'=8] {'mp'}, use_global_device_ids=true, to_apply=%add | all-reduce | flops 1024 | bytes 8192
  (81 shorter events, 8.0 us)
Async XLA Ops:
  7.2 102.4 %copy-start = (s32[2048,7]{0,1:T(8,128)S(1)}, s32[2048,7]{0,1:T(8,128)}, u32[]{:S(2)}) copy-start(s32[2048,7]{0,1:T(8,128)} %param.10) | copy-start | bytes 172036
  7.2 78.6 %copy-start.4 = (s32[2048]{0:T(1024)S(1)}, s32[2048]{0:T(1024)}, u32[]{:S(2)}) copy-start(s32[2048]{0:T(1024)} %param.12) | copy-start | bytes 24580
  7.2 101.8 %copy-start.3 = (s32[2048]{0:T(1024)S(1)}, s32[2048]{0:T(1024)}, u32[]{:S(2)}) copy-start(s32[2048]{0:T(1024)} %param.11) | copy-start | bytes 24580
  7.2 49.4 %copy-start.1 = (bf16[512,2048]{1,0:T(8,128)(2,1)S(1)}, bf16[512,2048]{1,0:T(8,128)(2,1)}, u32[]{:S(2)}) copy-start(bf16[512,2048]{1,0:T(8,128)(2,1)} %param.15) | copy-start | bytes 6291460
  7.2 102.9 %copy-start.5 = (f32[512]{0:T(512)S(1)}, f32[512]{0:T(512)}, u32[]{:S(2)}) copy-start(f32[512]{0:T(512)} %param.16) | copy-start | bytes 6148
  7.2 102.9 %copy-start.6 = (f32[512]{0:T(512)S(1)}, f32[512]{0:T(512)}, u32[]{:S(2)}) copy-start(f32[512]{0:T(512)} %param.17) | copy-start | bytes 6148
  7.2 102.9 %copy-start.7 = (f32[512]{0:T(512)S(1)}, f32[512]{0:T(512)}, u32[]{:S(2)}) copy-start(f32[512]{0:T(512)} %param.18) | copy-start | bytes 6148
  7.2 152.3 %all-gather.2.cloned.1.call-start = ((), (), s32[]{:S(2)}) async-start(), calls=%async_computation.3 | async-start | bytes 8650752 | tf_op jit(solution)/shard_map/all_gather | solution.py:80
  56.6 24.2 %collective-permute-start = (bf16[512,2048]{1,0:T(8,128)(2,1)S(1)}, bf16[512,2048]{1,0:T(8,128)(2,1)S(1)}, u32[]{:S(2)}, u32[]{:S(2)}) collective-permute-start(bf16[512,2048]{1,0:T(8,128)(2,1)S(1)} %copy-done.1), channel_id=1, source_target_pairs={{0,1},{1,2},{2,3},{3,4},{4,5},{5,6},{6,7},{7,0},{8,9},{9,10},{10,1... | collective-permute-start | bytes 6291464 | tf_op jit(solution)/shard_map/ppermute | solution.py:18
  57.9 25.8 %collective-permute-start.1 = (bf16[512,2048]{1,0:T(8,128)(2,1)S(1)}, bf16[512,2048]{1,0:T(8,128)(2,1)}, u32[]{:S(2)}, u32[]{:S(2)}) collective-permute-start(bf16[512,2048]{1,0:T(8,128)(2,1)S(1)} %copy-done.1), channel_id=1, source_target_pairs={{0,7},{1,0},{2,1},{3,2},{4,3},{5,4},{6,5},{7,6},{8,15},{9,8},{10,9... | collective-permute-start | bytes 6291464 | tf_op jit(solution)/shard_map/ppermute | solution.py:21
  80.8 2.8 %copy-start.2 = (bf16[512,2048]{1,0:T(8,128)(2,1)}, bf16[512,2048]{1,0:T(8,128)(2,1)S(1)}, u32[]{:S(2)}) copy-start(bf16[512,2048]{1,0:T(8,128)(2,1)S(1)} %collective-permute-done) | copy-start | bytes 6291460
  80.8 25.5 %collective-permute-start.2 = (bf16[512,2048]{1,0:T(8,128)(2,1)S(1)}, bf16[512,2048]{1,0:T(8,128)(2,1)}, u32[]{:S(2)}, u32[]{:S(2)}) collective-permute-start(bf16[512,2048]{1,0:T(8,128)(2,1)S(1)} %collective-permute-done), channel_id=1, source_target_pairs={{0,1},{1,2},{2,3},{3,4},{4,5},{5,6},{6,7},{7,0},{8,9},{9,10},{10,1... | collective-permute-start | bytes 6291464 | tf_op jit(solution)/shard_map/ppermute | solution.py:18
  83.6 26.8 %collective-permute-start.3 = (bf16[512,2048]{1,0:T(8,128)(2,1)}, bf16[512,2048]{1,0:T(8,128)(2,1)}, u32[]{:S(2)}, u32[]{:S(2)}) collective-permute-start(bf16[512,2048]{1,0:T(8,128)(2,1)} %collective-permute-done.1), channel_id=1, source_target_pairs={{0,7},{1,0},{2,1},{3,2},{4,3},{5,4},{6,5},{7,6},{8,15},{9,8},{10,9... | collective-permute-start | bytes 6291464 | tf_op jit(solution)/shard_map/ppermute | solution.py:21
  106.3 25.9 %collective-permute-start.4 = (bf16[512,2048]{1,0:T(8,128)(2,1)}, bf16[512,2048]{1,0:T(8,128)(2,1)}, u32[]{:S(2)}, u32[]{:S(2)}) collective-permute-start(bf16[512,2048]{1,0:T(8,128)(2,1)} %collective-permute-done.2), channel_id=1, source_target_pairs={{0,1},{1,2},{2,3},{3,4},{4,5},{5,6},{6,7},{7,0},{8,9},{9,10},{10,1... | collective-permute-start | bytes 6291464 | tf_op jit(solution)/shard_map/ppermute | solution.py:18
  110.4 25.0 %copy-start.10 = (u32[256]{0:T(256)S(1)}, u32[256]{0:T(256)}, u32[]{:S(2)}) copy-start(u32[256]{0:T(256)} %constant.108) | copy-start | bytes 3076
  110.4 43.2 %collective-permute-start.5 = (bf16[512,2048]{1,0:T(8,128)(2,1)}, bf16[512,2048]{1,0:T(8,128)(2,1)}, u32[]{:S(2)}, u32[]{:S(2)}) collective-permute-start(bf16[512,2048]{1,0:T(8,128)(2,1)} %collective-permute-done.3), channel_id=1, source_target_pairs={{0,7},{1,0},{2,1},{3,2},{4,3},{5,4},{6,5},{7,6},{8,15},{9,8},{10,9... | collective-permute-start | bytes 6291464 | tf_op jit(solution)/shard_map/ppermute | solution.py:21
  132.2 25.8 %collective-permute-start.6 = (bf16[512,2048]{1,0:T(8,128)(2,1)}, bf16[512,2048]{1,0:T(8,128)(2,1)S(1)}, u32[]{:S(2)}, u32[]{:S(2)}) collective-permute-start(bf16[512,2048]{1,0:T(8,128)(2,1)} %collective-permute-done.4), channel_id=1, source_target_pairs={{0,1},{1,2},{2,3},{3,4},{4,5},{5,6},{6,7},{7,0},{8,9},{9,10},{10,1... | collective-permute-start | bytes 6291464 | tf_op jit(solution)/shard_map/ppermute | solution.py:18
  183.7 39.7 %copy-start.8 = (f32[256]{0:T(256)S(1)}, f32[256]{0:T(256)}, u32[]{:S(2)}) copy-start(f32[256]{0:T(256)} %param.19) | copy-start | bytes 3076
  189.3 13.2 %all-to-all-start.2 = ((f32[3,32,32]{2,0,1:T(4,128)}), f32[3,32,32]{2,0,1:T(4,128)S(1)}, u32[]{:S(2)}, u32[]{:S(2)}) async-start(f32[3,32,32]{2,0,1:T(4,128)} %pad_maximum_fusion), calls=%async_computation.2 | async-start | bytes 131072 | tf_op jit(solution)/shard_map/all_to_all | solution.py:107
  223.2 1.2 copy-start.9
Sparse Core Ops, SparseCore 0:
  56.8 91.7 all-gather.1
